TPU v7x, 512 devices: a whole 4x8x8 slice. The times are simulated.
512 devices in a mesh: ctxlo: 16 (over z_hi, x), ctxhi: 32 (over y, z_lo, core).
Axes of the slice: x: 4, y: 8, z: 8 (z_hi: 4, z_lo: 2; z = z_hi * 2 + z_lo), core: 2. Of those that a mesh axis runs over, the one named last changes fastest.
Arguments:
- key_value: bfloat16 [32, 16, 384, 256], P('ctxhi', 'ctxlo'), may hold values from -6 to 6
- queries: bfloat16 [32, 16, 384, 768], P('ctxhi', 'ctxlo'), may hold values from -300 to 300
Outputs:
- attended: bfloat16 [32, 16, 384, 768], P('ctxhi', 'ctxlo')
All inputs are finite; a program needn't handle non-finite values.
Results may differ from a plain program's by a relative error of at most 0.0038.
Values may be sent and summed in bfloat16 or wider, within the bound.
No kernel may reach another device: no remote copies, remote signals or barrier semaphores. Data moves between devices by JAX's collectives and lax.ppermute only.
A program may use at most 64 MiB of HBM per device.

v0:
```python
import math

import jax
import jax.numpy as jnp
from jax import lax
from jax.sharding import PartitionSpec as P

HQ = 6


def swapped(block, axis, stride):
    count = lax.axis_size(axis)
    route = []
    for low in range(count):
        high = low | 1 << stride
        if high != low and high < count:
            route += [(low, high), (high, low)]
    return lax.ppermute(block, axis, route)


def per_device(key_value, queries):
    tokens = key_value.shape[2]
    pair = key_value.shape[3]
    head_size = pair // 2
    local_kv = key_value.reshape(tokens, pair)
    query = queries.reshape(tokens, HQ, head_size)
    scale = 1.0 / math.sqrt(head_size)

    def absorb(state, block):
        top, total, summed = state
        scores = (
            jnp.einsum(
                "thd,sd->hts", query, block[:, :head_size], preferred_element_type=jnp.float32
            )
            * scale
        )
        new_top = jnp.maximum(top, jnp.max(scores, axis=-1))
        fade = jnp.exp(top - new_top)
        expo = jnp.exp(scores - new_top[:, :, None])
        total = total * fade + jnp.sum(expo, axis=-1)
        weights = expo.astype(jnp.bfloat16)
        update = jnp.einsum(
            "hts,sd->thd", weights, block[:, head_size:], preferred_element_type=jnp.float32
        )
        summed = summed * jnp.transpose(fade)[:, :, None] + update
        return (new_top, total, summed)

    start_state = (
        jnp.full((HQ, tokens), -1e30, jnp.float32),
        jnp.zeros((HQ, tokens), jnp.float32),
        jnp.zeros((tokens, HQ, head_size), jnp.float32),
    )
    state = absorb(start_state, local_kv)
    near_state = state
    low_bits = lax.axis_size("ctxlo").bit_length() - 1
    for bit in range(low_bits):
        near_state = absorb(near_state, swapped(local_kv, "ctxlo", bit))
    state = near_state
    for bit in range(lax.axis_size("ctxhi").bit_length() - 1):
        state = absorb(state, swapped(local_kv, "ctxhi", bit))
    top, total, summed = state
    result = summed / jnp.transpose(total)[:, :, None]
    return result.astype(jnp.bfloat16).reshape(1, 1, tokens, HQ * head_size)


def solution(mesh):
    return jax.shard_map(
        per_device,
        mesh=mesh,
        in_specs=(P("ctxhi", "ctxlo", None, None), P("ctxhi", "ctxlo", None, None)),
        out_specs=P("ctxhi", "ctxlo", None, None),
        check_vma=False,
    )
```

profile of v0, /device:TPU:8, one launch (start us, length us, event | category | flops | bytes accessed | tf_op | source)
XLA Modules:
  0.0 72.8 jit_solution(15755119193530976494)
XLA Ops:
  0.0 0.0 copy-start.1
  0.0 2.0 %collective-permute-start.4 = (bf16[384,256]{1,0:T(8,128)(2,1)}, bf16[384,256]{1,0:T(8,128)(2,1)S(1)}, u32[]{:S(2)}, u32[]{:S(2)}) collective-permute-start(bf16[384,256]{1,0:T(8,128)(2,1)} %bitcast.469), channel_id=1, source_target_pairs={{0,1},{1,0},{2,3},{3,2},{4,5},{5,4},{6,7},{7,6},{8,9},{9,8},{10,11... | collective-permute-start | bytes 589832 | tf_op jit(solution)/shard_map/ppermute | solution.py:18
  2.1 6.1 %collective-permute-start.2 = (bf16[384,256]{1,0:T(8,128)(2,1)}, bf16[384,256]{1,0:T(8,128)(2,1)S(1)}, u32[]{:S(2)}, u32[]{:S(2)}) collective-permute-start(bf16[384,256]{1,0:T(8,128)(2,1)} %bitcast.470), channel_id=1, source_target_pairs={{0,128},{128,0},{32,160},{160,32},{64,192},{192,64},{96,224},{224,... | collective-permute-start | bytes 589832 | tf_op jit(solution)/shard_map/ppermute | solution.py:18
  8.2 3.4 %collective-permute-start = (bf16[384,256]{1,0:T(8,128)(2,1)}, bf16[384,256]{1,0:T(8,128)(2,1)S(1)}, u32[]{:S(2)}, u32[]{:S(2)}) collective-permute-start(bf16[384,256]{1,0:T(8,128)(2,1)} %bitcast.471), channel_id=1, source_target_pairs={{0,32},{32,0},{64,96},{96,64},{128,160},{160,128},{192,224},{224,1... | collective-permute-start | bytes 589832 | tf_op jit(solution)/shard_map/ppermute | solution.py:18
  11.6 6.8 %collective-permute-start.8 = (bf16[384,256]{1,0:T(8,128)(2,1)}, bf16[384,256]{1,0:T(8,128)(2,1)S(1)}, u32[]{:S(2)}, u32[]{:S(2)}) collective-permute-start(bf16[384,256]{1,0:T(8,128)(2,1)} %bitcast.472), channel_id=1, source_target_pairs={{0,16},{16,0},{1,17},{17,1},{2,18},{18,2},{3,19},{19,3},{4,20},{20... | collective-permute-start | bytes 589832 | tf_op jit(solution)/shard_map/ppermute | solution.py:18
  18.4 2.7 %collective-permute-start.7 = (bf16[384,256]{1,0:T(8,128)(2,1)}, bf16[384,256]{1,0:T(8,128)(2,1)S(1)}, u32[]{:S(2)}, u32[]{:S(2)}) collective-permute-start(bf16[384,256]{1,0:T(8,128)(2,1)} %bitcast.473), channel_id=1, source_target_pairs={{0,8},{8,0},{1,9},{9,1},{2,10},{10,2},{3,11},{11,3},{4,12},{12,4},... | collective-permute-start | bytes 589832 | tf_op jit(solution)/shard_map/ppermute | solution.py:18
  21.1 1.4 %copy.34 = bf16[1,1,384,768]{2,3,1,0:T(8,128)(2,1)S(1)} copy(bf16[1,1,384,768]{3,2,1,0:T(8,128)(2,1)} %param.3) | data formatting | bytes 1179648 | tf_op args[1]
  22.5 1.5 %bitcast_reduce_fusion.9 = (f32[6,384]{1,0:T(8,128)S(1)}, f32[384,384,6]{1,0,2:T(8,128)S(1)}) fusion(bf16[384,6,128]{0,2,1:T(8,128)(2,1)S(1)} %bitcast.458, bf16[384,256]{1,0:T(8,128)(2,1)} %bitcast.474), kind=kOutput, calls=%fused_computation.28 | convolution fusion | flops 228259584 | bytes 4236288 | tf_op jit(solution)/shard_map/thd,sd->hts/dot_general | solution.py:32
  24.0 0.0 collective-permute-done.4
  24.0 0.0 copy-done.1
  24.0 3.3 %collective-permute-start.6 = (bf16[384,256]{1,0:T(8,128)(2,1)S(1)}, bf16[384,256]{1,0:T(8,128)(2,1)S(1)}, u32[]{:S(2)}, u32[]{:S(2)}) collective-permute-start(bf16[384,256]{1,0:T(8,128)(2,1)S(1)} %bitcast.475), channel_id=1, source_target_pairs={{0,4},{4,0},{1,5},{5,1},{2,6},{6,2},{3,7},{7,3},{8,12},{12,8},{9,1... | collective-permute-start | bytes 589832 | tf_op jit(solution)/shard_map/ppermute | solution.py:18
  27.3 0.6 bitcast_reduce_fusion.4
  27.9 0.0 collective-permute-done.2
  27.9 4.3 %collective-permute-start.5 = (bf16[384,256]{1,0:T(8,128)(2,1)S(1)}, bf16[384,256]{1,0:T(8,128)(2,1)S(1)}, u32[]{:S(2)}, u32[]{:S(2)}) collective-permute-start(bf16[384,256]{1,0:T(8,128)(2,1)S(1)} %bitcast.476), channel_id=1, source_target_pairs={{0,2},{2,0},{1,3},{3,1},{4,6},{6,4},{5,7},{7,5},{8,10},{10,8},{9,1... | collective-permute-start | bytes 589832 | tf_op jit(solution)/shard_map/ppermute | solution.py:18
  32.2 0.6 bitcast_reduce_fusion.6
  32.8 0.0 collective-permute-done
  32.8 8.2 %collective-permute-start.3 = (bf16[384,256]{1,0:T(8,128)(2,1)S(1)}, bf16[384,256]{1,0:T(8,128)(2,1)S(1)}, u32[]{:S(2)}, u32[]{:S(2)}) collective-permute-start(bf16[384,256]{1,0:T(8,128)(2,1)S(1)} %bitcast.477), channel_id=1, source_target_pairs={{0,256},{256,0},{32,288},{288,32},{64,320},{320,64},{96,352},{352,... | collective-permute-start | bytes 589832 | tf_op jit(solution)/shard_map/ppermute | solution.py:18
  41.0 2.4 %bitcast_reduce_fusion.8 = (f32[6,384]{1,0:T(8,128)S(1)}, f32[384,384,6]{1,0,2:T(8,128)}) fusion(bf16[384,6,128]{0,2,1:T(8,128)(2,1)S(1)} %bitcast.461, bf16[384,256]{1,0:T(8,128)(2,1)S(1)} %collective-permute-done), kind=kOutput, calls=%fused_computation.25 | convolution fusion | flops 228259584 | bytes 4236288 | tf_op jit(solution)/shard_map/thd,sd->hts/dot_general | solution.py:32
  43.4 0.0 collective-permute-done.8
  43.4 4.8 %collective-permute-start.1 = (bf16[384,256]{1,0:T(8,128)(2,1)S(1)}, bf16[384,256]{1,0:T(8,128)(2,1)S(1)}, u32[]{:S(2)}, u32[]{:S(2)}) collective-permute-start(bf16[384,256]{1,0:T(8,128)(2,1)S(1)} %bitcast.478), channel_id=1, source_target_pairs={{0,64},{64,0},{32,96},{96,32},{128,192},{192,128},{160,224},{224,1... | collective-permute-start | bytes 589832 | tf_op jit(solution)/shard_map/ppermute | solution.py:18
  48.2 0.6 bitcast_reduce_fusion
  48.8 0.0 collective-permute-done.7
  48.9 0.6 bitcast_reduce_fusion.1
  49.5 0.0 collective-permute-done.5
  49.5 0.6 bitcast_reduce_fusion.3
  50.1 0.7 collective-permute-done.3
  50.8 0.6 bitcast_reduce_fusion.5
  51.4 1.1 %collective-permute-done.1 = bf16[384,256]{1,0:T(8,128)(2,1)S(1)} collective-permute-done((bf16[384,256]{1,0:T(8,128)(2,1)S(1)}, bf16[384,256]{1,0:T(8,128)(2,1)S(1)}, u32[]{:S(2)}, u32[]{:S(2)}) %collective-permute-start.1) | collective-permute-done | bytes 196640 | tf_op jit(solution)/shard_map/ppermute | solution.py:18
  52.5 0.6 bitcast_reduce_fusion.7
  53.1 0.0 collective-permute-done.6
  53.1 0.6 bitcast_reduce_fusion.2
  53.8 3.2 %fusion.10 = (f32[6,384]{1,0:T(8,128)S(1)}, f32[6,384]{1,0:T(8,128)S(1)}) fusion(f32[384,384,6]{1,0,2:T(8,128)S(1)} %get-tuple-element.48, f32[6,384]{1,0:T(8,128)S(1)} %get-tuple-element.28, f32[6,384]{1,0:T(8,128)S(1)} %get-tuple-element.25, f32[384,384,6]{1,0,2:T(8,128)} %get-tuple-element.46), kind=kLoop, calls=%fused_computation.30 | loop fusion | flops 5303808 | bytes 7114752 | tf_op jit(solution)/shard_map/reduce_sum | solution.py:40
  57.0 0.8 %fusion.76 = f32[384,6,128]{0,2,1:T(8,128)S(1)} fusion(f32[384,384,6]{1,0,2:T(8,128)S(1)} %get-tuple-element.48, f32[6,384]{1,0:T(8,128)S(1)} %get-tuple-element.28, f32[384,6]{0,1:T(8,128)S(1)} %get-tuple-element.26, f32[384,6]{0,1:T(8,128)S(1)} %get-tuple-element.27, bf16[384,256]{1,0:T(8,128)(2,1)S(1)} %bitcast.479), kind=kOutput, calls=%fused_computation.82 | convolution fusion | flops 229736448 | bytes 4853760 | tf_op jit(solution)/shard_map/hts,sd->thd/dot_general | solution.py:42
  57.8 1.2 %fusion.14 = (f32[6,384]{1,0:T(8,128)S(1)}, f32[6,384]{1,0:T(8,128)S(1)}) fusion(f32[384,384,6]{1,0,2:T(8,128)S(1)} %get-tuple-element.44, f32[6,384]{1,0:T(8,128)S(1)} %get-tuple-element.24, f32[6,384]{1,0:T(8,128)S(1)} %get-tuple-element.23, f32[384,384,6]{1,0,2:T(8,128)S(1)} %get-tuple-element.42), kind=kLoop, calls=%fused_computation.34 | loop fusion | flops 5303808 | bytes 7114752 | tf_op jit(solution)/shard_map/reduce_sum | solution.py:40
  58.9 1.2 %fusion.18 = (f32[6,384]{1,0:T(8,128)S(1)}, f32[6,384]{1,0:T(8,128)S(1)}) fusion(f32[384,384,6]{1,0,2:T(8,128)S(1)} %get-tuple-element.40, f32[6,384]{1,0:T(8,128)S(1)} %get-tuple-element.22, f32[6,384]{1,0:T(8,128)S(1)} %get-tuple-element.21, f32[384,384,6]{1,0,2:T(8,128)S(1)} %get-tuple-element.38), kind=kLoop, calls=%fused_computation.38 | loop fusion | flops 5303808 | bytes 7114752 | tf_op jit(solution)/shard_map/reduce_sum | solution.py:40
  60.1 1.2 %fusion.22 = (f32[6,384]{1,0:T(8,128)S(1)}, f32[6,384]{1,0:T(8,128)S(1)}) fusion(f32[384,384,6]{1,0,2:T(8,128)S(1)} %get-tuple-element.36, f32[6,384]{1,0:T(8,128)S(1)} %get-tuple-element.20, f32[6,384]{1,0:T(8,128)S(1)} %get-tuple-element.19, f32[384,384,6]{1,0,2:T(8,128)S(1)} %get-tuple-element.34), kind=kLoop, calls=%fused_computation.42 | loop fusion | flops 5303808 | bytes 7114752 | tf_op jit(solution)/shard_map/reduce_sum | solution.py:40
  61.3 1.2 %fusion.26 = (f32[6,384]{1,0:T(8,128)S(1)}, f32[6,384]{1,0:T(8,128)S(1)}) fusion(f32[384,384,6]{1,0,2:T(8,128)S(1)} %get-tuple-element.32, f32[6,384]{1,0:T(8,128)S(1)} %get-tuple-element.18, f32[6,384]{1,0:T(8,128)S(1)} %get-tuple-element.17, f32[384,384,6]{1,0,2:T(8,128)S(1)} %get-tuple-element.30), kind=kLoop, calls=%fused_computation.46 | loop fusion | flops 5303808 | bytes 7114752 | tf_op jit(solution)/shard_map/reduce_sum | solution.py:40
  62.5 0.1 bitcast_add_fusion
  62.6 0.8 %fusion.100 = f32[384,6,128]{0,2,1:T(8,128)S(1)} fusion(f32[384,384,6]{1,0,2:T(8,128)S(1)} %get-tuple-element.38, f32[6,384]{1,0:T(8,128)S(1)} %get-tuple-element.21, bf16[384,256]{1,0:T(8,128)(2,1)S(1)} %collective-permute-done.4), kind=kOutput, calls=%fused_computation.90 | convolution fusion | flops 229146624 | bytes 4829184 | tf_op jit(solution)/shard_map/hts,sd->thd/dot_general | solution.py:42
  63.3 0.8 %fusion.91 = f32[384,6,128]{0,2,1:T(8,128)S(1)} fusion(f32[384,384,6]{1,0,2:T(8,128)S(1)} %get-tuple-element.44, f32[6,384]{1,0:T(8,128)S(1)} %get-tuple-element.24, bf16[384,256]{1,0:T(8,128)(2,1)S(1)} %collective-permute-done.1), kind=kOutput, calls=%fused_computation.87 | convolution fusion | flops 229146624 | bytes 4829184 | tf_op jit(solution)/shard_map/hts,sd->thd/dot_general | solution.py:42
  64.1 1.0 %fusion.94 = f32[384,6,128]{0,2,1:T(8,128)S(1)} fusion(f32[384,384,6]{1,0,2:T(8,128)S(1)} %get-tuple-element.42, f32[6,384]{1,0:T(8,128)S(1)} %get-tuple-element.23, bf16[384,256]{1,0:T(8,128)(2,1)S(1)} %collective-permute-done.2), kind=kOutput, calls=%fused_computation.88 | convolution fusion | flops 229146624 | bytes 4829184 | tf_op jit(solution)/shard_map/hts,sd->thd/dot_general | solution.py:42
  65.1 0.8 %fusion.97 = f32[384,6,128]{0,2,1:T(8,128)S(1)} fusion(f32[384,384,6]{1,0,2:T(8,128)S(1)} %get-tuple-element.40, f32[6,384]{1,0:T(8,128)S(1)} %get-tuple-element.22, bf16[384,256]{1,0:T(8,128)(2,1)S(1)} %collective-permute-done.3), kind=kOutput, calls=%fused_computation.89 | convolution fusion | flops 229146624 | bytes 4829184 | tf_op jit(solution)/shard_map/hts,sd->thd/dot_general | solution.py:42
  65.9 0.8 %fusion.103 = f32[384,6,128]{0,2,1:T(8,128)S(1)} fusion(f32[384,384,6]{1,0,2:T(8,128)S(1)} %get-tuple-element.36, f32[6,384]{1,0:T(8,128)S(1)} %get-tuple-element.20, bf16[384,256]{1,0:T(8,128)(2,1)S(1)} %collective-permute-done.5), kind=kOutput, calls=%fused_computation.91 | convolution fusion | flops 229146624 | bytes 4829184 | tf_op jit(solution)/shard_map/hts,sd->thd/dot_general | solution.py:42
  66.7 0.8 %fusion.106 = f32[384,6,128]{0,2,1:T(8,128)S(1)} fusion(f32[384,384,6]{1,0,2:T(8,128)S(1)} %get-tuple-element.34, f32[6,384]{1,0:T(8,128)S(1)} %get-tuple-element.19, bf16[384,256]{1,0:T(8,128)(2,1)S(1)} %collective-permute-done.6), kind=kOutput, calls=%fused_computation.92 | convolution fusion | flops 229146624 | bytes 4829184 | tf_op jit(solution)/shard_map/hts,sd->thd/dot_general | solution.py:42
  67.4 0.8 %fusion.109 = f32[384,6,128]{0,2,1:T(8,128)S(1)} fusion(f32[384,384,6]{1,0,2:T(8,128)S(1)} %get-tuple-element.32, f32[6,384]{1,0:T(8,128)S(1)} %get-tuple-element.18, bf16[384,256]{1,0:T(8,128)(2,1)S(1)} %collective-permute-done.7), kind=kOutput, calls=%fused_computation.93 | convolution fusion | flops 229146624 | bytes 4829184 | tf_op jit(solution)/shard_map/hts,sd->thd/dot_general | solution.py:42
  68.2 0.0 copy-start
  68.2 0.8 %fusion.112 = f32[384,6,128]{0,2,1:T(8,128)S(1)} fusion(f32[384,384,6]{1,0,2:T(8,128)S(1)} %get-tuple-element.30, f32[6,384]{1,0:T(8,128)S(1)} %get-tuple-element.17, bf16[384,256]{1,0:T(8,128)(2,1)S(1)} %collective-permute-done.8), kind=kOutput, calls=%fused_computation.94 | convolution fusion | flops 229146624 | bytes 4829184 | tf_op jit(solution)/shard_map/hts,sd->thd/dot_general | solution.py:42
  69.0 1.2 %copy-done = f32[384,384,6]{1,0,2:T(8,128)S(1)} copy-done((f32[384,384,6]{1,0,2:T(8,128)S(1)}, f32[384,384,6]{1,0,2:T(8,128)}, u32[]{:S(2)}) %copy-start) | copy-done | bytes 3538968
  70.2 1.5 %fusion.160 = bf16[384,6,128]{0,2,1:T(8,128)(2,1)S(1)} fusion(f32[384,6,128]{0,2,1:T(8,128)S(1)} %fusion.112, f32[384,6,128]{0,2,1:T(8,128)S(1)} %fusion.109, f32[384,6,128]{0,2,1:T(8,128)S(1)} %fusion.106, f32[384,6,128]{0,2,1:T(8,128)S(1)} %fusion.103, f32[384,6,128]{0,2,1:T(8,128)S(1)} %fusion.100, f32[384,6,128]{0,2,1:T(8,128)S(1)} %fusion.97, ...), kind=kOutput, calls=%fused_computation.110 | convolution fusion | flops 234749952 | bytes 14966784 | tf_op jit(solution)/shard_map/hts,sd->thd/dot_general | solution.py:42
  71.7 1.1 %copy.65 = bf16[1,1,384,768]{3,2,1,0:T(8,128)(2,1)} copy(bf16[1,1,384,768]{2,3,1,0:T(8,128)(2,1)S(1)} %bitcast.468) | data formatting | bytes 1179648 | tf_op jit(solution)/shard_map/reshape | solution.py:63
  (2 shorter events, 0.0 us)
Async XLA Ops:
  0.0 24.0 %copy-start.1 = (bf16[1,1,384,256]{3,2,1,0:T(8,128)(2,1)S(1)}, bf16[1,1,384,256]{3,2,1,0:T(8,128)(2,1)}, u32[]{:S(2)}) copy-start(bf16[1,1,384,256]{3,2,1,0:T(8,128)(2,1)} %param.2) | copy-start | bytes 589828
  0.0 24.0 %collective-permute-start.4 = (bf16[384,256]{1,0:T(8,128)(2,1)}, bf16[384,256]{1,0:T(8,128)(2,1)S(1)}, u32[]{:S(2)}, u32[]{:S(2)}) collective-permute-start(bf16[384,256]{1,0:T(8,128)(2,1)} %bitcast.469), channel_id=1, source_target_pairs={{0,1},{1,0},{2,3},{3,2},{4,5},{5,4},{6,7},{7,6},{8,9},{9,8},{10,11... | collective-permute-start | bytes 589832 | tf_op jit(solution)/shard_map/ppermute | solution.py:18
  2.1 25.9 %collective-permute-start.2 = (bf16[384,256]{1,0:T(8,128)(2,1)}, bf16[384,256]{1,0:T(8,128)(2,1)S(1)}, u32[]{:S(2)}, u32[]{:S(2)}) collective-permute-start(bf16[384,256]{1,0:T(8,128)(2,1)} %bitcast.470), channel_id=1, source_target_pairs={{0,128},{128,0},{32,160},{160,32},{64,192},{192,64},{96,224},{224,... | collective-permute-start | bytes 589832 | tf_op jit(solution)/shard_map/ppermute | solution.py:18
  8.2 24.7 %collective-permute-start = (bf16[384,256]{1,0:T(8,128)(2,1)}, bf16[384,256]{1,0:T(8,128)(2,1)S(1)}, u32[]{:S(2)}, u32[]{:S(2)}) collective-permute-start(bf16[384,256]{1,0:T(8,128)(2,1)} %bitcast.471), channel_id=1, source_target_pairs={{0,32},{32,0},{64,96},{96,64},{128,160},{160,128},{192,224},{224,1... | collective-permute-start | bytes 589832 | tf_op jit(solution)/shard_map/ppermute | solution.py:18
  11.6 31.8 %collective-permute-start.8 = (bf16[384,256]{1,0:T(8,128)(2,1)}, bf16[384,256]{1,0:T(8,128)(2,1)S(1)}, u32[]{:S(2)}, u32[]{:S(2)}) collective-permute-start(bf16[384,256]{1,0:T(8,128)(2,1)} %bitcast.472), channel_id=1, source_target_pairs={{0,16},{16,0},{1,17},{17,1},{2,18},{18,2},{3,19},{19,3},{4,20},{20... | collective-permute-start | bytes 589832 | tf_op jit(solution)/shard_map/ppermute | solution.py:18
  18.4 30.4 %collective-permute-start.7 = (bf16[384,256]{1,0:T(8,128)(2,1)}, bf16[384,256]{1,0:T(8,128)(2,1)S(1)}, u32[]{:S(2)}, u32[]{:S(2)}) collective-permute-start(bf16[384,256]{1,0:T(8,128)(2,1)} %bitcast.473), channel_id=1, source_target_pairs={{0,8},{8,0},{1,9},{9,1},{2,10},{10,2},{3,11},{11,3},{4,12},{12,4},... | collective-permute-start | bytes 589832 | tf_op jit(solution)/shard_map/ppermute | solution.py:18
  24.0 29.1 %collective-permute-start.6 = (bf16[384,256]{1,0:T(8,128)(2,1)S(1)}, bf16[384,256]{1,0:T(8,128)(2,1)S(1)}, u32[]{:S(2)}, u32[]{:S(2)}) collective-permute-start(bf16[384,256]{1,0:T(8,128)(2,1)S(1)} %bitcast.475), channel_id=1, source_target_pairs={{0,4},{4,0},{1,5},{5,1},{2,6},{6,2},{3,7},{7,3},{8,12},{12,8},{9,1... | collective-permute-start | bytes 589832 | tf_op jit(solution)/shard_map/ppermute | solution.py:18
  27.9 21.6 %collective-permute-start.5 = (bf16[384,256]{1,0:T(8,128)(2,1)S(1)}, bf16[384,256]{1,0:T(8,128)(2,1)S(1)}, u32[]{:S(2)}, u32[]{:S(2)}) collective-permute-start(bf16[384,256]{1,0:T(8,128)(2,1)S(1)} %bitcast.476), channel_id=1, source_target_pairs={{0,2},{2,0},{1,3},{3,1},{4,6},{6,4},{5,7},{7,5},{8,10},{10,8},{9,1... | collective-permute-start | bytes 589832 | tf_op jit(solution)/shard_map/ppermute | solution.py:18
  32.8 18.0 %collective-permute-start.3 = (bf16[384,256]{1,0:T(8,128)(2,1)S(1)}, bf16[384,256]{1,0:T(8,128)(2,1)S(1)}, u32[]{:S(2)}, u32[]{:S(2)}) collective-permute-start(bf16[384,256]{1,0:T(8,128)(2,1)S(1)} %bitcast.477), channel_id=1, source_target_pairs={{0,256},{256,0},{32,288},{288,32},{64,320},{320,64},{96,352},{352,... | collective-permute-start | bytes 589832 | tf_op jit(solution)/shard_map/ppermute | solution.py:18
  43.4 9.1 %collective-permute-start.1 = (bf16[384,256]{1,0:T(8,128)(2,1)S(1)}, bf16[384,256]{1,0:T(8,128)(2,1)S(1)}, u32[]{:S(2)}, u32[]{:S(2)}) collective-permute-start(bf16[384,256]{1,0:T(8,128)(2,1)S(1)} %bitcast.478), channel_id=1, source_target_pairs={{0,64},{64,0},{32,96},{96,32},{128,192},{192,128},{160,224},{224,1... | collective-permute-start | bytes 589832 | tf_op jit(solution)/shard_map/ppermute | solution.py:18
  68.2 2.0 %copy-start = (f32[384,384,6]{1,0,2:T(8,128)S(1)}, f32[384,384,6]{1,0,2:T(8,128)}, u32[]{:S(2)}) copy-start(f32[384,384,6]{1,0,2:T(8,128)} %get-tuple-element.46) | copy-start | bytes 10616836
where the time goes:
time: 73.3 us; the launch traced here: 72.8 us
  starting transfers between devices  41.6 us (57%)
  matrix products  17.4 us (24%)
  other arithmetic  8.02 us (11%)
  local copies, waits for them, and re-layouts  3.67 us (5%)
  waiting for transfers between devices  1.78 us (2%)
    ppermute x9, starting transfers between devices, swapped(): return lax.ppermute(block, axis, route)  41.6 us
    dot_general x10, matrix products, absorb(): jnp.einsum('thd,sd->hts', query, block[:, :head_size], preferred_element_...  8.77 us
    dot_general x10, matrix products, absorb(): jnp.einsum('hts,sd->thd', weights, block[:, head_size:], preferred_elemen...  8.62 us
    reduce_sum x5, other arithmetic, absorb(): total = total * fade + jnp.sum(expo, axis=-1)  7.93 us
    unnamed x5, local copies, waits for them, and re-layouts  2.59 us
    ppermute x9, waiting for transfers between devices, swapped(): return lax.ppermute(block, axis, route)  1.78 us
  transfers between devices with their start and end apart: 9, of which 2 were waited for; matrix products, arithmetic and copies ran while one was open for 13% of the time, Pallas kernels for 0%

commit v1 on v0

v1 whole, which is shorter than its diff:
```python
import math

import jax
import jax.numpy as jnp
from jax import lax
from jax.experimental import pallas as pl
from jax.experimental.pallas import tpu as pltpu
from jax.sharding import PartitionSpec as P

HQ = 6


def swapped(block, axis, stride):
    count = lax.axis_size(axis)
    route = []
    for low in range(count):
        high = low | 1 << stride
        if high != low and high < count:
            route += [(low, high), (high, low)]
    return lax.ppermute(block, axis, route)


def attend_kernel(*refs):
    q_ref = refs[0]
    kv_refs = refs[1:-2]
    o_ref, s_ref = refs[-2], refs[-1]
    tokens = q_ref.shape[0]
    head_size = q_ref.shape[1]
    scale = 1.0 / math.sqrt(head_size)
    query = q_ref[...]
    for j, kv_ref in enumerate(kv_refs):
        keys = kv_ref[:, :head_size]
        scores = lax.dot_general(
            query, keys, (((1,), (1,)), ((), ())), preferred_element_type=jnp.float32
        )
        s_ref[:, j * tokens:(j + 1) * tokens] = scores * scale
    scores = s_ref[...]
    top = jnp.max(scores, axis=-1, keepdims=True)
    expo = jnp.exp(scores - top)
    total = jnp.sum(expo, axis=-1, keepdims=True)
    weights = expo.astype(jnp.bfloat16)
    summed = jnp.zeros((tokens, head_size), jnp.float32)
    for j, kv_ref in enumerate(kv_refs):
        summed = summed + jnp.dot(
            weights[:, j * tokens:(j + 1) * tokens],
            kv_ref[:, head_size:],
            preferred_element_type=jnp.float32,
        )
    o_ref[...] = (summed / total).astype(o_ref.dtype)


def attend(query, blocks):
    tokens, width = query.shape
    head_size = blocks[0].shape[1] // 2
    kv_spec = pl.BlockSpec(blocks[0].shape, lambda h: (0, 0))
    return pl.pallas_call(
        attend_kernel,
        out_shape=jax.ShapeDtypeStruct((tokens, width), jnp.bfloat16),
        grid=(width // head_size,),
        in_specs=[pl.BlockSpec((tokens, head_size), lambda h: (0, h))] + [kv_spec] * len(blocks),
        out_specs=pl.BlockSpec((tokens, head_size), lambda h: (0, h)),
        scratch_shapes=[pltpu.VMEM((tokens, tokens * len(blocks)), jnp.float32)],
    )(query, *blocks)


def per_device(key_value, queries):
    tokens = key_value.shape[2]
    pair = key_value.shape[3]
    local_kv = key_value.reshape(tokens, pair)
    query = queries.reshape(tokens, queries.shape[3])
    blocks = [local_kv]
    for bit in range(lax.axis_size("ctxlo").bit_length() - 1):
        blocks.append(swapped(local_kv, "ctxlo", bit))
    for bit in range(lax.axis_size("ctxhi").bit_length() - 1):
        blocks.append(swapped(local_kv, "ctxhi", bit))
    result = attend(query, blocks)
    return result.reshape(1, 1, tokens, queries.shape[3])


def solution(mesh):
    return jax.shard_map(
        per_device,
        mesh=mesh,
        in_specs=(P("ctxhi", "ctxlo", None, None), P("ctxhi", "ctxlo", None, None)),
        out_specs=P("ctxhi", "ctxlo", None, None),
        check_vma=False,
    )
```

time: 73.3 us -> 69.8 us (0.952)
  the two profiles are of different devices: /device:TPU:8 before, /device:TPU:1 now
where the time goes in v1:
time: 69.8 us; the launch traced here: 69.5 us
  starting transfers between devices  41.3 us (59%)
  Pallas kernels  19.7 us (28%)
  waiting for transfers between devices  7.44 us (11%)
  local copies, waits for them, and re-layouts  0.78 us (1%)
    ppermute x9, starting transfers between devices, swapped(): return lax.ppermute(block, axis, route)  41.3 us
    pallas_call x1, Pallas kernels, attend(): pl.pallas_call(attend_kernel, out_shape=jax.ShapeDtypeStruct((tokens, wid...  19.7 us
    ppermute x9, waiting for transfers between devices, swapped(): return lax.ppermute(block, axis, route)  7.44 us
  transfers between devices with their start and end apart: 9, of which 1 were waited for; matrix products, arithmetic and copies ran while one was open for 0% of the time, Pallas kernels for 0%

profile of v1, /device:TPU:1, one launch (start us, length us, event | category | flops | bytes accessed | tf_op | source)
XLA Modules:
  0.0 69.5 jit_solution(4802330952456816363)
XLA Ops:
  0.0 8.3 %collective-permute-start.8 = (bf16[384,256]{1,0:T(8,128)(2,1)}, bf16[384,256]{1,0:T(8,128)(2,1)S(1)}, u32[]{:S(2)}, u32[]{:S(2)}) collective-permute-start(bf16[384,256]{1,0:T(8,128)(2,1)} %bitcast.4), channel_id=1, source_target_pairs={{0,16},{16,0},{1,17},{17,1},{2,18},{18,2},{3,19},{19,3},{4,20},{20... | collective-permute-start | bytes 589832 | tf_op jit(solution)/shard_map/ppermute | solution.py:20
  8.3 2.4 %collective-permute-start.7 = (bf16[384,256]{1,0:T(8,128)(2,1)}, bf16[384,256]{1,0:T(8,128)(2,1)S(1)}, u32[]{:S(2)}, u32[]{:S(2)}) collective-permute-start(bf16[384,256]{1,0:T(8,128)(2,1)} %bitcast.5), channel_id=1, source_target_pairs={{0,8},{8,0},{1,9},{9,1},{2,10},{10,2},{3,11},{11,3},{4,12},{12,4},... | collective-permute-start | bytes 589832 | tf_op jit(solution)/shard_map/ppermute | solution.py:20
  10.7 2.3 %collective-permute-start.6 = (bf16[384,256]{1,0:T(8,128)(2,1)}, bf16[384,256]{1,0:T(8,128)(2,1)S(1)}, u32[]{:S(2)}, u32[]{:S(2)}) collective-permute-start(bf16[384,256]{1,0:T(8,128)(2,1)} %bitcast.6), channel_id=1, source_target_pairs={{0,4},{4,0},{1,5},{5,1},{2,6},{6,2},{3,7},{7,3},{8,12},{12,8},{9,1... | collective-permute-start | bytes 589832 | tf_op jit(solution)/shard_map/ppermute | solution.py:20
  13.0 4.0 %collective-permute-start.5 = (bf16[384,256]{1,0:T(8,128)(2,1)}, bf16[384,256]{1,0:T(8,128)(2,1)S(1)}, u32[]{:S(2)}, u32[]{:S(2)}) collective-permute-start(bf16[384,256]{1,0:T(8,128)(2,1)} %bitcast.7), channel_id=1, source_target_pairs={{0,2},{2,0},{1,3},{3,1},{4,6},{6,4},{5,7},{7,5},{8,10},{10,8},{9,1... | collective-permute-start | bytes 589832 | tf_op jit(solution)/shard_map/ppermute | solution.py:20
  17.0 3.7 %collective-permute-start.4 = (bf16[384,256]{1,0:T(8,128)(2,1)}, bf16[384,256]{1,0:T(8,128)(2,1)S(1)}, u32[]{:S(2)}, u32[]{:S(2)}) collective-permute-start(bf16[384,256]{1,0:T(8,128)(2,1)} %bitcast.8), channel_id=1, source_target_pairs={{0,1},{1,0},{2,3},{3,2},{4,5},{5,4},{6,7},{7,6},{8,9},{9,8},{10,11... | collective-permute-start | bytes 589832 | tf_op jit(solution)/shard_map/ppermute | solution.py:20
  20.7 0.0 collective-permute-done.8.refs_10_
  20.7 0.0 copy-start
  20.8 9.7 %collective-permute-start.3 = (bf16[384,256]{1,0:T(8,128)(2,1)}, bf16[384,256]{1,0:T(8,128)(2,1)S(1)}, u32[]{:S(2)}, u32[]{:S(2)}) collective-permute-start(bf16[384,256]{1,0:T(8,128)(2,1)} %bitcast.9), channel_id=1, source_target_pairs={{0,256},{256,0},{32,288},{288,32},{64,320},{320,64},{96,352},{352,... | collective-permute-start | bytes 589832 | tf_op jit(solution)/shard_map/ppermute | solution.py:20
  30.5 0.0 collective-permute-done.7.refs_9_
  30.5 0.0 copy-start.1
  30.5 4.0 %collective-permute-start.2 = (bf16[384,256]{1,0:T(8,128)(2,1)}, bf16[384,256]{1,0:T(8,128)(2,1)S(1)}, u32[]{:S(2)}, u32[]{:S(2)}) collective-permute-start(bf16[384,256]{1,0:T(8,128)(2,1)} %bitcast.10), channel_id=1, source_target_pairs={{0,128},{128,0},{32,160},{160,32},{64,192},{192,64},{96,224},{224,... | collective-permute-start | bytes 589832 | tf_op jit(solution)/shard_map/ppermute | solution.py:20
  34.5 0.0 collective-permute-done.6.refs_8_
  34.6 0.0 copy-start.2
  34.6 4.7 %collective-permute-start.1 = (bf16[384,256]{1,0:T(8,128)(2,1)}, bf16[384,256]{1,0:T(8,128)(2,1)S(1)}, u32[]{:S(2)}, u32[]{:S(2)}) collective-permute-start(bf16[384,256]{1,0:T(8,128)(2,1)} %bitcast.11), channel_id=1, source_target_pairs={{0,64},{64,0},{32,96},{96,32},{128,192},{192,128},{160,224},{224,1... | collective-permute-start | bytes 589832 | tf_op jit(solution)/shard_map/ppermute | solution.py:20
  39.2 0.0 collective-permute-done.5.refs_7_
  39.2 0.0 copy-start.3
  39.2 2.2 %collective-permute-start = (bf16[384,256]{1,0:T(8,128)(2,1)}, bf16[384,256]{1,0:T(8,128)(2,1)S(1)}, u32[]{:S(2)}, u32[]{:S(2)}) collective-permute-start(bf16[384,256]{1,0:T(8,128)(2,1)} %bitcast.12), channel_id=1, source_target_pairs={{0,32},{32,0},{64,96},{96,64},{128,160},{160,128},{192,224},{224,1... | collective-permute-start | bytes 589832 | tf_op jit(solution)/shard_map/ppermute | solution.py:20
  41.5 0.0 collective-permute-done.4.refs_6_
  41.5 0.0 copy-start.4
  41.5 0.0 collective-permute-done.3.refs_5_
  41.5 0.0 copy-start.5
  41.5 7.4 %collective-permute-done.2.refs_4_ = bf16[384,256]{1,0:T(8,128)(2,1)S(1)} collective-permute-done((bf16[384,256]{1,0:T(8,128)(2,1)}, bf16[384,256]{1,0:T(8,128)(2,1)S(1)}, u32[]{:S(2)}, u32[]{:S(2)}) %collective-permute-start.2) | collective-permute-done | bytes 196640 | tf_op jit(solution)/shard_map/ppermute | solution.py:20
  48.9 0.0 copy-start.6
  48.9 0.0 collective-permute-done.1.refs_3_
  48.9 0.0 copy-start.7
  48.9 0.0 collective-permute-done.refs_2_
  48.9 0.0 copy-start.8
  49.0 0.0 copy-done
  49.0 0.0 copy-done.1
  49.0 0.0 copy-done.2
  49.0 0.0 copy-done.3
  49.0 0.0 copy-done.4
  49.0 0.0 copy-done.5
  49.0 0.6 copy-done.6
  49.6 0.1 copy-done.7
  49.7 0.1 copy-done.8
  49.8 19.7 %shard_map.28 = bf16[384,768]{1,0:T(8,128)(2,1)} custom-call(bf16[384,768]{1,0:T(8,128)(2,1)} %bitcast.3, bf16[384,256]{1,0:T(8,128)(2,1)} %bitcast.13, bf16[384,256]{1,0:T(8,128)(2,1)} %copy-done.8, bf16[384,256]{1,0:T(8,128)(2,1)} %copy-done.7, bf16[384,256]{1,0:T(8,128)(2,1)} %copy-done.6, bf16[384,256]{1,0:T(8,128)(2,1)} %copy-done.5, ...), custom_call_target="tpu_custom_call" | custom-call | tf_op jit(solution)/shard_map/pallas_call | solution.py:56
Async XLA Ops:
  0.0 20.7 %collective-permute-start.8 = (bf16[384,256]{1,0:T(8,128)(2,1)}, bf16[384,256]{1,0:T(8,128)(2,1)S(1)}, u32[]{:S(2)}, u32[]{:S(2)}) collective-permute-start(bf16[384,256]{1,0:T(8,128)(2,1)} %bitcast.4), channel_id=1, source_target_pairs={{0,16},{16,0},{1,17},{17,1},{2,18},{18,2},{3,19},{19,3},{4,20},{20... | collective-permute-start | bytes 589832 | tf_op jit(solution)/shard_map/ppermute | solution.py:20
  8.3 22.2 %collective-permute-start.7 = (bf16[384,256]{1,0:T(8,128)(2,1)}, bf16[384,256]{1,0:T(8,128)(2,1)S(1)}, u32[]{:S(2)}, u32[]{:S(2)}) collective-permute-start(bf16[384,256]{1,0:T(8,128)(2,1)} %bitcast.5), channel_id=1, source_target_pairs={{0,8},{8,0},{1,9},{9,1},{2,10},{10,2},{3,11},{11,3},{4,12},{12,4},... | collective-permute-start | bytes 589832 | tf_op jit(solution)/shard_map/ppermute | solution.py:20
  10.7 23.8 %collective-permute-start.6 = (bf16[384,256]{1,0:T(8,128)(2,1)}, bf16[384,256]{1,0:T(8,128)(2,1)S(1)}, u32[]{:S(2)}, u32[]{:S(2)}) collective-permute-start(bf16[384,256]{1,0:T(8,128)(2,1)} %bitcast.6), channel_id=1, source_target_pairs={{0,4},{4,0},{1,5},{5,1},{2,6},{6,2},{3,7},{7,3},{8,12},{12,8},{9,1... | collective-permute-start | bytes 589832 | tf_op jit(solution)/shard_map/ppermute | solution.py:20
  13.0 26.2 %collective-permute-start.5 = (bf16[384,256]{1,0:T(8,128)(2,1)}, bf16[384,256]{1,0:T(8,128)(2,1)S(1)}, u32[]{:S(2)}, u32[]{:S(2)}) collective-permute-start(bf16[384,256]{1,0:T(8,128)(2,1)} %bitcast.7), channel_id=1, source_target_pairs={{0,2},{2,0},{1,3},{3,1},{4,6},{6,4},{5,7},{7,5},{8,10},{10,8},{9,1... | collective-permute-start | bytes 589832 | tf_op jit(solution)/shard_map/ppermute | solution.py:20
  17.0 24.4 %collective-permute-start.4 = (bf16[384,256]{1,0:T(8,128)(2,1)}, bf16[384,256]{1,0:T(8,128)(2,1)S(1)}, u32[]{:S(2)}, u32[]{:S(2)}) collective-permute-start(bf16[384,256]{1,0:T(8,128)(2,1)} %bitcast.8), channel_id=1, source_target_pairs={{0,1},{1,0},{2,3},{3,2},{4,5},{5,4},{6,7},{7,6},{8,9},{9,8},{10,11... | collective-permute-start | bytes 589832 | tf_op jit(solution)/shard_map/ppermute | solution.py:20
  20.7 28.2 %copy-start = (bf16[384,256]{1,0:T(8,128)(2,1)}, bf16[384,256]{1,0:T(8,128)(2,1)S(1)}, u32[]{:S(2)}) copy-start(bf16[384,256]{1,0:T(8,128)(2,1)S(1)} %collective-permute-done.8.refs_10_) | copy-start | bytes 589828
  20.8 20.7 %collective-permute-start.3 = (bf16[384,256]{1,0:T(8,128)(2,1)}, bf16[384,256]{1,0:T(8,128)(2,1)S(1)}, u32[]{:S(2)}, u32[]{:S(2)}) collective-permute-start(bf16[384,256]{1,0:T(8,128)(2,1)} %bitcast.9), channel_id=1, source_target_pairs={{0,256},{256,0},{32,288},{288,32},{64,320},{320,64},{96,352},{352,... | collective-permute-start | bytes 589832 | tf_op jit(solution)/shard_map/ppermute | solution.py:20
  30.5 18.5 %copy-start.1 = (bf16[384,256]{1,0:T(8,128)(2,1)}, bf16[384,256]{1,0:T(8,128)(2,1)S(1)}, u32[]{:S(2)}) copy-start(bf16[384,256]{1,0:T(8,128)(2,1)S(1)} %collective-permute-done.7.refs_9_) | copy-start | bytes 589828
  30.5 18.4 %collective-permute-start.2 = (bf16[384,256]{1,0:T(8,128)(2,1)}, bf16[384,256]{1,0:T(8,128)(2,1)S(1)}, u32[]{:S(2)}, u32[]{:S(2)}) collective-permute-start(bf16[384,256]{1,0:T(8,128)(2,1)} %bitcast.10), channel_id=1, source_target_pairs={{0,128},{128,0},{32,160},{160,32},{64,192},{192,64},{96,224},{224,... | collective-permute-start | bytes 589832 | tf_op jit(solution)/shard_map/ppermute | solution.py:20
  34.6 14.4 %copy-start.2 = (bf16[384,256]{1,0:T(8,128)(2,1)}, bf16[384,256]{1,0:T(8,128)(2,1)S(1)}, u32[]{:S(2)}) copy-start(bf16[384,256]{1,0:T(8,128)(2,1)S(1)} %collective-permute-done.6.refs_8_) | copy-start | bytes 589828
  34.6 14.4 %collective-permute-start.1 = (bf16[384,256]{1,0:T(8,128)(2,1)}, bf16[384,256]{1,0:T(8,128)(2,1)S(1)}, u32[]{:S(2)}, u32[]{:S(2)}) collective-permute-start(bf16[384,256]{1,0:T(8,128)(2,1)} %bitcast.11), channel_id=1, source_target_pairs={{0,64},{64,0},{32,96},{96,32},{128,192},{192,128},{160,224},{224,1... | collective-permute-start | bytes 589832 | tf_op jit(solution)/shard_map/ppermute | solution.py:20
  39.2 9.8 %copy-start.3 = (bf16[384,256]{1,0:T(8,128)(2,1)}, bf16[384,256]{1,0:T(8,128)(2,1)S(1)}, u32[]{:S(2)}) copy-start(bf16[384,256]{1,0:T(8,128)(2,1)S(1)} %collective-permute-done.5.refs_7_) | copy-start | bytes 589828
  39.2 9.7 %collective-permute-start = (bf16[384,256]{1,0:T(8,128)(2,1)}, bf16[384,256]{1,0:T(8,128)(2,1)S(1)}, u32[]{:S(2)}, u32[]{:S(2)}) collective-permute-start(bf16[384,256]{1,0:T(8,128)(2,1)} %bitcast.12), channel_id=1, source_target_pairs={{0,32},{32,0},{64,96},{96,64},{128,160},{160,128},{192,224},{224,1... | collective-permute-start | bytes 589832 | tf_op jit(solution)/shard_map/ppermute | solution.py:20
  41.5 7.5 %copy-start.4 = (bf16[384,256]{1,0:T(8,128)(2,1)}, bf16[384,256]{1,0:T(8,128)(2,1)S(1)}, u32[]{:S(2)}) copy-start(bf16[384,256]{1,0:T(8,128)(2,1)S(1)} %collective-permute-done.4.refs_6_) | copy-start | bytes 589828
  41.5 7.5 %copy-start.5 = (bf16[384,256]{1,0:T(8,128)(2,1)}, bf16[384,256]{1,0:T(8,128)(2,1)S(1)}, u32[]{:S(2)}) copy-start(bf16[384,256]{1,0:T(8,128)(2,1)S(1)} %collective-permute-done.3.refs_5_) | copy-start | bytes 589828
  48.9 0.7 copy-start.6
  48.9 0.8 %copy-start.7 = (bf16[384,256]{1,0:T(8,128)(2,1)}, bf16[384,256]{1,0:T(8,128)(2,1)S(1)}, u32[]{:S(2)}) copy-start(bf16[384,256]{1,0:T(8,128)(2,1)S(1)} %collective-permute-done.1.refs_3_) | copy-start | bytes 589828
  48.9 0.8 %copy-start.8 = (bf16[384,256]{1,0:T(8,128)(2,1)}, bf16[384,256]{1,0:T(8,128)(2,1)S(1)}, u32[]{:S(2)}) copy-start(bf16[384,256]{1,0:T(8,128)(2,1)S(1)} %collective-permute-done.refs_2_) | copy-start | bytes 589828

commit v2 on v1

v2 whole, which is shorter than its diff:
```python
import math

import jax
import jax.numpy as jnp
from jax import lax
from jax.experimental import pallas as pl
from jax.experimental.pallas import tpu as pltpu
from jax.sharding import Mesh, PartitionSpec as P

HQ = 6


def bit_names(prefix, count):
    return tuple(f"{prefix}{b}" for b in reversed(range(count.bit_length() - 1)))


def attend_kernel(sel_ref, *refs):
    q_ref = refs[0]
    kv_refs = refs[1:-2]
    o_ref, s_ref = refs[-2], refs[-1]
    tokens = q_ref.shape[0]
    head_size = q_ref.shape[1]
    scale = 1.0 / math.sqrt(head_size)
    query = q_ref[...]
    for j, kv_ref in enumerate(kv_refs):
        keys = kv_ref[:, :head_size]
        scores = lax.dot_general(
            query, keys, (((1,), (1,)), ((), ())), preferred_element_type=jnp.float32
        )
        s_ref[:, j * tokens:(j + 1) * tokens] = scores * scale
    scores = s_ref[...]
    top = jnp.max(scores, axis=-1, keepdims=True)
    expo = jnp.exp(scores - top)
    total = jnp.sum(expo, axis=-1, keepdims=True)
    weights = expo.astype(jnp.bfloat16)
    summed = jnp.zeros((tokens, head_size), jnp.float32)
    for j, kv_ref in enumerate(kv_refs):
        summed = summed + jnp.dot(
            weights[:, j * tokens:(j + 1) * tokens],
            kv_ref[:, head_size:],
            preferred_element_type=jnp.float32,
        )
    o_ref[...] = (summed / total).astype(o_ref.dtype)


def attend(query, local, picks):
    tokens, width = query.shape
    head_size = local.shape[1] // 2
    sel = jnp.stack([index for _, index in picks]).astype(jnp.int32)
    local_spec = pl.BlockSpec(local.shape, lambda h, s: (0, 0))
    specs = [pl.BlockSpec((tokens, head_size), lambda h, s: (0, h)), local_spec]
    for i, _ in enumerate(picks):
        specs.append(pl.BlockSpec((None,) + local.shape, lambda h, s, i=i: (s[i], 0, 0)))
    grid_spec = pltpu.PrefetchScalarGridSpec(
        num_scalar_prefetch=1,
        grid=(width // head_size,),
        in_specs=specs,
        out_specs=pl.BlockSpec((tokens, head_size), lambda h, s: (0, h)),
        scratch_shapes=[pltpu.VMEM((tokens, tokens * (len(picks) + 1)), jnp.float32)],
    )
    return pl.pallas_call(
        attend_kernel,
        out_shape=jax.ShapeDtypeStruct((tokens, width), jnp.bfloat16),
        grid_spec=grid_spec,
    )(sel, query, local, *[gathered for gathered, _ in picks])


def make_per_device(groups):
    def per_device(key_value, queries):
        tokens = key_value.shape[2]
        pair = key_value.shape[3]
        local_kv = key_value.reshape(tokens, pair)
        query = queries.reshape(tokens, queries.shape[3])
        picks = []
        for names in groups:
            gathered = lax.all_gather(local_kv, names)
            me = lax.axis_index(names)
            for b in range(len(names)):
                picks.append((gathered, jnp.bitwise_xor(me, 1 << b)))
        result = attend(query, local_kv, picks)
        return result.reshape(1, 1, tokens, queries.shape[3])
    return per_device


def solution(mesh):
    hi = bit_names("h", mesh.shape["ctxhi"])
    lo = bit_names("l", mesh.shape["ctxlo"])
    names = {"ctxhi": hi, "ctxlo": lo}
    order = sum((names[axis] for axis in mesh.axis_names), ())
    binary = Mesh(mesh.devices.reshape((2,) * len(order)), order)
    groups = [lo[i:i + 2] for i in range(0, len(lo), 2)]
    groups += [hi[::-1][i:i + 2][::-1] for i in range(0, len(hi), 2)]
    spec = P(hi, lo, None, None)
    return jax.shard_map(
        make_per_device(groups),
        mesh=binary,
        in_specs=(spec, spec),
        out_specs=spec,
        check_vma=False,
    )
```

time: 69.8 us -> 108 us (1.55)
  the two profiles are of different devices: /device:TPU:1 before, /device:TPU:6 now
where the time goes in v2:
time: 108 us
  blocking collectives  86.4 us (80%)
  Pallas kernels  20.6 us (19%)
    all_gather x5, blocking collectives, per_device(): gathered = lax.all_gather(local_kv, names)  86.4 us
    pallas_call x1, Pallas kernels, attend(): pl.pallas_call(attend_kernel, out_shape=jax.ShapeDtypeStruct((tokens, wid...  20.6 us

profile of v2, /device:TPU:6, one launch (start us, length us, event | category | flops | bytes accessed | tf_op | source)
XLA Modules:
  0.0 107.6 jit_solution(6428619312723833710)
XLA Ops:
  0.0 0.6 stack.39.sel_ref
  0.6 0.0 copy-start
  0.6 18.4 %all-gather.4 = bf16[2,1,384,256]{3,2,1,0:T(8,128)(2,1)} all-gather(bf16[1,1,384,256]{3,2,1,0:T(8,128)(2,1)} %param.2), channel_id=6, replica_groups=mesh['l3'=2,'l2'=2,'l1'=2,'l0'=2,'h4'=2,'h3'=2,'h2'=2,'h1'=2,'h0'=2] {'h4'}, dimensions={0}, use_global_device_ids=true | all-gather | bytes 589824 | tf_op jit(solution)/shard_map/all_gather | solution.py:76
  19.0 0.0 copy-done
  19.0 18.5 %all-gather.3 = bf16[4,1,384,256]{3,2,1,0:T(8,128)(2,1)} all-gather(bf16[1,1,384,256]{3,2,1,0:T(8,128)(2,1)S(1)} %copy-done), channel_id=5, replica_groups=mesh['l3'=2,'l2'=2,'l1'=2,'l0'=2,'h4'=2,'h3'=2,'h2'=2,'h1'=2,'h0'=2] {'h..., dimensions={0}, use_global_device_ids=true | all-gather | bytes 983040 | tf_op jit(solution)/shard_map/all_gather | solution.py:76
  37.5 9.9 %all-gather.2 = bf16[4,1,384,256]{3,2,1,0:T(8,128)(2,1)} all-gather(bf16[1,1,384,256]{3,2,1,0:T(8,128)(2,1)S(1)} %copy-done), channel_id=4, replica_groups=mesh['l3'=2,'l2'=2,'l1'=2,'l0'=2,'h4'=2,'h3'=2,'h2'=2,'h1'=2,'h0'=2] {'h..., dimensions={0}, use_global_device_ids=true | all-gather | bytes 983040 | tf_op jit(solution)/shard_map/all_gather | solution.py:76
  47.4 15.2 %all-gather.1 = bf16[4,1,384,256]{3,2,1,0:T(8,128)(2,1)} all-gather(bf16[1,1,384,256]{3,2,1,0:T(8,128)(2,1)S(1)} %copy-done), channel_id=3, replica_groups=mesh['l3'=2,'l2'=2,'l1'=2,'l0'=2,'h4'=2,'h3'=2,'h2'=2,'h1'=2,'h0'=2] {'l..., dimensions={0}, use_global_device_ids=true | all-gather | bytes 983040 | tf_op jit(solution)/shard_map/all_gather | solution.py:76
  62.6 24.4 %all-gather = bf16[4,1,384,256]{3,2,1,0:T(8,128)(2,1)} all-gather(bf16[1,1,384,256]{3,2,1,0:T(8,128)(2,1)S(1)} %copy-done), channel_id=2, replica_groups=mesh['l3'=2,'l2'=2,'l1'=2,'l0'=2,'h4'=2,'h3'=2,'h2'=2,'h1'=2,'h0'=2] {'l..., dimensions={0}, use_global_device_ids=true | all-gather | bytes 983040 | tf_op jit(solution)/shard_map/all_gather | solution.py:76
  87.0 20.6 %shard_map.28 = bf16[384,768]{1,0:T(8,128)(2,1)} custom-call(s32[9]{0:T(128)} %stack.39.sel_ref, bf16[384,768]{1,0:T(8,128)(2,1)} %bitcast.27, bf16[384,256]{1,0:T(8,128)(2,1)} %bitcast.17, bf16[4,384,256]{2,1,0:T(8,128)(2,1)} %bitcast.24, bf16[4,384,256]{2,1,0:T(8,128)(2,1)} %bitcast.25, bf16[4,384,256]{2,1,0:T(8,128)(2,1)} %bitcast.22, ...), custom_call_target="tpu_custom_call" | custom-call | tf_op jit(solution)/shard_map/pallas_call | solution.py:61
Async XLA Ops:
  0.6 18.4 %copy-start = (bf16[1,1,384,256]{3,2,1,0:T(8,128)(2,1)S(1)}, bf16[1,1,384,256]{3,2,1,0:T(8,128)(2,1)}, u32[]{:S(2)}) copy-start(bf16[1,1,384,256]{3,2,1,0:T(8,128)(2,1)} %param.2) | copy-start | bytes 589828
